TPU v7x, 256 devices: a whole 4x4x8 slice. The times are simulated.
256 devices in a mesh: dp: 32 (over z_hi, y, core), mp: 8 (over x, z_lo).
Axes of the slice: x: 4, y: 4, z: 8 (z_hi: 4, z_lo: 2; z = z_hi * 2 + z_lo), core: 2. Of those that a mesh axis runs over, the one named last changes fastest.
Arguments:
- activations: bfloat16 [2, 64, 384, 14336], P(None, 'dp', None, 'mp'), may hold values from -6 to 6
- out_grads: bfloat16 [2, 64, 384, 4096], P(None, 'dp', None, 'mp'), may hold values from -6 to 6
- proj_in: bfloat16 [14336, 64], P('mp'), may hold values from -0.046875 to 0.046875
- proj_out: bfloat16 [4096, 64], P('mp'), may hold values from -0.09375 to 0.09375
- store: bfloat16 [2, 65536, 4096], P(None, ('dp', 'mp')), may hold values from -0.09375 to 0.09375
- ckpt_rate: float32 [2], replicated, may hold values from 0.5 to 2
- store_group: int32 [65536], P(('dp', 'mp')), may hold values from 0 to 15
Outputs:
- scores: float32 [64, 65536], P(None, ('dp', 'mp'))
- group_scores: float32 [64, 16], replicated
All inputs are finite; a program needn't handle non-finite values.
Results may differ from a plain program's by a relative error of at most 0.005.
Values may be sent and summed in bfloat16 or wider, within the bound.
No kernel may reach another device: no remote copies, remote signals or barrier semaphores. Data moves between devices by JAX's collectives and lax.ppermute only.
A program may use at most 64 MiB of HBM per device.

v0:
```python
import jax
import jax.numpy as jnp
from jax import lax
from jax.sharding import PartitionSpec as P

GROUPS = 16


def shards(activations, out_grads, proj_in, proj_out, store, ckpt_rate, store_group):
    rank = proj_in.shape[1]
    seq_len = activations.shape[2]
    ex_local = activations.shape[1]
    scale = 1.0 / jnp.sqrt(jnp.float32(seq_len))
    part_in = jnp.einsum("cesf,fr->cesr", activations, proj_in, preferred_element_type=jnp.float32)
    part_out = jnp.einsum("cesf,fr->cesr", out_grads, proj_out, preferred_element_type=jnp.float32)
    stacked = jnp.concatenate([part_in, part_out], axis=3)
    summed = lax.psum(stacked, "mp")
    low_in = summed[..., :rank].astype(jnp.bfloat16)
    low_grad = summed[..., rank:].astype(jnp.bfloat16)
    outer = jnp.einsum("cesa,cesb->ecab", low_in, low_grad, preferred_element_type=jnp.float32)
    query = (outer.reshape(ex_local, 2, rank * rank) * scale).astype(jnp.bfloat16)
    piece = lax.all_gather(query, "dp", axis=0, tiled=True)
    first = jnp.einsum("qk,rk->qr", piece[:, 0], store[0], preferred_element_type=jnp.float32)
    second = jnp.einsum("qk,rk->qr", piece[:, 1], store[1], preferred_element_type=jnp.float32)
    scores = ckpt_rate[0] * first + ckpt_rate[1] * second
    member = (store_group[:, None] == jnp.arange(GROUPS, dtype=jnp.int32)[None, :]).astype(
        jnp.float32
    )
    partial_totals = jnp.dot(scores, member, precision=lax.Precision.HIGHEST)
    totals = lax.psum(partial_totals, ("dp", "mp"))
    store_rows = store.shape[1] * lax.axis_size("dp") * lax.axis_size("mp")
    group_scores = totals / jnp.sqrt(jnp.float32(store_rows) / jnp.float32(GROUPS))
    return (scores, group_scores)


def solution(mesh):
    placed = (
        P(None, "dp", None, "mp"),
        P(None, "dp", None, "mp"),
        P("mp", None),
        P("mp", None),
        P(None, ("dp", "mp"), None),
        P(),
        P(("dp", "mp")),
    )
    return jax.shard_map(
        shards, mesh=mesh, in_specs=placed, out_specs=(P(None, ("dp", "mp")), P()), check_vma=False
    )
```

profile of v0, /device:TPU:1, one launch (start us, length us, event | category | flops | bytes accessed | tf_op | source)
XLA Modules:
  0.0 203.9 jit_solution(9762679956642732704)
XLA Ops:
  7.2 0.0 copy-start
  7.2 0.0 copy-start.1
  7.2 0.0 all-gather.2.cloned.1.call-start
  7.2 4.4 %fusion.16 = f32[2,2,384,64]{2,3,1,0:T(8,128)S(1)} fusion(bf16[2,2,384,1792]{3,2,1,0:T(8,128)(2,1)} %param.7, bf16[1792,64]{0,1:T(8,128)(2,1)} %param.9), kind=kOutput, calls=%fused_computation.14 | convolution fusion | flops 352321536 | bytes 6127616 | tf_op jit(solution)/shard_map/cesf,fr->cesr/dot_general | solution.py:14
  11.7 0.0 copy-done
  11.7 0.0 copy-done.1
  11.7 0.0 copy-start.3
  11.7 0.6 fusion.21
  12.3 0.1 pad_maximum_fusion
  12.4 43.3 %all-reduce.1 = bf16[2,2,384,128]{2,3,1,0:T(8,128)(2,1)S(1)} all-reduce(f32[2,2,384,128]{2,3,1,0:T(8,128)S(1)} %pad_maximum_fusion), channel_id=1, replica_groups=mesh['dp'=32,'mp'=8] {'mp'}, use_global_device_ids=true, to_apply=%region_0.0 | all-reduce | flops 196608 | bytes 1179648 | tf_op jit(solution)/shard_map/psum | solution.py:17
  55.7 0.2 fusion.6
  55.9 0.7 convert_element_type.10
  56.7 0.0 all-gather.2.cloned.1.call-update
  56.7 0.0 copy-done.3
  56.7 0.6 fusion.26
  57.3 57.2 %all-gather.2.cloned.1.call-done = bf16[64,2,4096]{2,1,0:T(2,128)(2,1)} async-done(((bf16[2,2,4096]{2,1,0:T(2,128)(2,1)}), bf16[64,2,4096]{2,1,0:T(2,128)(2,1)}) %all-gather.2.cloned.1.call-update) | async-done | bytes 1048592 | tf_op jit(solution)/shard_map/all_gather | solution.py:22
  114.6 3.7 %fusion.24 = (bf16[64,1,4096]{2,1,0:T(2,128)(2,1)S(1)}, bf16[64,1,4096]{2,1,0:T(2,128)(2,1)S(1)}) fusion(bf16[64,2,4096]{2,1,0:T(2,128)(2,1)} %all-gather.2.cloned.1.call-done), kind=kLoop, calls=%fused_computation.24 | loop fusion | bytes 2097152 | tf_op jit(solution)/shard_map/slice | solution.py:23
  118.3 0.0 copy-done.5
  118.3 1.6 fusion.13
  119.9 1.6 fusion.10
  121.5 0.0 copy-start.2
  121.5 0.3 fusion.20
  121.8 74.6 %psum.15 = f32[64,16]{0,1:T(8,128)S(1)} all-reduce(f32[64,16]{0,1:T(8,128)S(1)} %fusion.20), channel_id=1, replica_groups=mesh['dp'=32,'mp'=8] {'dp','mp'}, use_global_device_ids=true, to_apply=%region_1.0 | all-reduce | flops 1024 | bytes 8192 | tf_op jit(solution)/shard_map/psum | solution.py:30
  196.4 0.6 broadcast_multiply_fusion
  (5 shorter events, 0.1 us)
Async XLA Ops:
  7.2 4.5 %copy-start = (bf16[2,2,384,512]{3,2,1,0:T(8,128)(2,1)S(1)}, bf16[2,2,384,512]{3,2,1,0:T(8,128)(2,1)}, u32[]{:S(2)}) copy-start(bf16[2,2,384,512]{3,2,1,0:T(8,128)(2,1)} %param.8) | copy-start | bytes 4718596
  7.2 4.5 %copy-start.1 = (bf16[512,64]{0,1:T(8,128)(2,1)S(1)}, bf16[512,64]{0,1:T(8,128)(2,1)}, u32[]{:S(2)}) copy-start(bf16[512,64]{0,1:T(8,128)(2,1)} %param.10) | copy-start | bytes 196612
  7.2 107.4 %all-gather.2.cloned.1.call-start = ((), (), s32[]{:S(2)}) async-start(), calls=%async_computation | async-start | bytes 1081344 | tf_op jit(solution)/shard_map/all_gather | solution.py:22
  11.7 45.0 %copy-start.3 = (f32[2]{0:T(128)S(1)}, f32[2]{0:T(128)}, u32[]{:S(2)}) copy-start(f32[2]{0:T(128)} %param.12) | copy-start | bytes 28
  57.3 64.1 %copy-start.4 = (s32[256]{0:T(256)S(1)}, s32[256]{0:T(256)}, u32[]{:S(2)}) copy-start(s32[256]{0:T(256)} %param.13) | copy-start | bytes 3076
  114.6 3.7 %copy-start.5 = (bf16[2,256,4096]{2,1,0:T(8,128)(2,1)S(1)}, bf16[2,256,4096]{2,1,0:T(8,128)(2,1)}, u32[]{:S(2)}) copy-start(bf16[2,256,4096]{2,1,0:T(8,128)(2,1)} %param.11) | copy-start | bytes 12582916
  121.5 75.6 %copy-start.2 = (f32[64,256]{1,0:T(8,128)}, f32[64,256]{1,0:T(8,128)S(1)}, u32[]{:S(2)}) copy-start(f32[64,256]{1,0:T(8,128)S(1)} %fusion.10) | copy-start | bytes 196612
Sparse Core Ops, SparseCore 0:
  56.8 57.6 all-gather.1
where the time goes:
time: 204 us
  blocking collectives  118 us (58%)
  waiting for transfers between devices  57.3 us (28%)
  between operations  14.2 us (7%)
  matrix products  8.67 us (4%)
  local copies, waits for them, and re-layouts  5.12 us (3%)
    psum x1, blocking collectives, shards(): totals = lax.psum(partial_totals, ('dp', 'mp'))  74.6 us
    all_gather x1, waiting for transfers between devices, shards(): piece = lax.all_gather(query, 'dp', axis=0, tiled=True)  57.2 us
    psum x1, blocking collectives, shards(): summed = lax.psum(stacked, 'mp')  43.3 us
    dot_general x1, matrix products, shards(): jnp.einsum('cesf,fr->cesr', activations, proj_in, preferred_element_type=...  4.43 us
  transfers between devices with their start and end apart: 1, of which 1 were waited for; matrix products, arithmetic and copies ran while one was open for 0% of the time, Pallas kernels for 0%

commit v1 on v0

--- a/solution.py
+++ b/solution.py
@@ -4,6 +4,13 @@
 from jax.sharding import PartitionSpec as P
 
 GROUPS = 16
+
+
+def derive_rails(vector):
+    return jnp.concatenate(
+        lax.all_to_all(jnp.stack([vector for _ in range(lax.axis_size("dp"))], axis=0), "dp", 0, 0),
+        axis=0,
+    )
 
 
 def shards(activations, out_grads, proj_in, proj_out, store, ckpt_rate, store_group):
@@ -19,7 +26,7 @@
     low_grad = summed[..., rank:].astype(jnp.bfloat16)
     outer = jnp.einsum("cesa,cesb->ecab", low_in, low_grad, preferred_element_type=jnp.float32)
     query = (outer.reshape(ex_local, 2, rank * rank) * scale).astype(jnp.bfloat16)
-    piece = lax.all_gather(query, "dp", axis=0, tiled=True)
+    piece = derive_rails(query)
     first = jnp.einsum("qk,rk->qr", piece[:, 0], store[0], preferred_element_type=jnp.float32)
     second = jnp.einsum("qk,rk->qr", piece[:, 1], store[1], preferred_element_type=jnp.float32)
     scores = ckpt_rate[0] * first + ckpt_rate[1] * second

time: 204 us -> 180 us (0.88)
  waiting for transfers between devices: 57.3 us -> 28 us
  starting transfers between devices: 0.04 us -> 15.8 us
  between operations: 14.2 us -> 0.76 us
  matrix products: 8.67 us -> 11.6 us
    all_gather x1 -> x0, waiting for transfers between devices: 57.2 us -> none  [shards(): piece = lax.all_gather(query, 'dp', axis=0, tiled=True)]
    all_to_all x0 -> x1, waiting for transfers between devices: none -> 28 us  [derive_rails(): lax.all_to_all(jnp.stack([vector for _ in range(lax.axis_size('dp'))], ax...]
    all_to_all x0 -> x1, starting transfers between devices: none -> 15.8 us  [derive_rails(): lax.all_to_all(jnp.stack([vector for _ in range(lax.axis_size('dp'))], ax...]
    slice x1 -> x0, local copies, waits for them, and re-layouts: 3.7 us -> none  [shards(): piece[:, 0]]
where the time goes in v1:
time: 180 us
  blocking collectives  117 us (65%)
  waiting for transfers between devices  28 us (16%)
  starting transfers between devices  15.8 us (9%)
  matrix products  11.6 us (6%)
  local copies, waits for them, and re-layouts  6.15 us (3%)
    psum x1, blocking collectives, shards(): totals = lax.psum(partial_totals, ('dp', 'mp'))  73.6 us
    psum x1, blocking collectives, shards(): summed = lax.psum(stacked, 'mp')  43.3 us
    all_to_all x1, waiting for transfers between devices, derive_rails(): lax.all_to_all(jnp.stack([vector for _ in range(lax.axis_size('dp'))], ax...  28 us
    all_to_all x1, starting transfers between devices, derive_rails(): lax.all_to_all(jnp.stack([vector for _ in range(lax.axis_size('dp'))], ax...  15.8 us
    dot_general x1, matrix products, shards(): jnp.einsum('cesf,fr->cesr', activations, proj_in, preferred_element_type=...  4.44 us
  transfers between devices with their start and end apart: 1, of which 1 were waited for; matrix products, arithmetic and copies ran while one was open for 0% of the time, Pallas kernels for 0%

profile of v1, /device:TPU:1, one launch (start us, length us, event | category | flops | bytes accessed | tf_op | source)
XLA Modules:
  0.0 179.8 jit_solution(1642637515930545417)
XLA Ops:
  0.6 0.0 copy-start
  0.6 0.0 copy-start.1
  0.7 4.4 %fusion.16 = f32[2,2,384,64]{2,3,1,0:T(8,128)S(1)} fusion(bf16[2,2,384,1792]{3,2,1,0:T(8,128)(2,1)} %param.7, bf16[1792,64]{0,1:T(8,128)(2,1)} %param.9), kind=kOutput, calls=%fused_computation.14 | convolution fusion | flops 352321536 | bytes 6127616 | tf_op jit(solution)/shard_map/cesf,fr->cesr/dot_general | solution.py:21
  5.1 0.0 copy-done
  5.1 0.0 copy-done.1
  5.1 0.6 fusion.21
  5.7 0.0 copy-start.3
  5.7 0.1 pad_maximum_fusion
  5.8 43.3 %all-reduce.1 = bf16[2,2,384,128]{2,3,1,0:T(8,128)(2,1)S(1)} all-reduce(f32[2,2,384,128]{2,3,1,0:T(8,128)S(1)} %pad_maximum_fusion), channel_id=1, replica_groups=mesh['dp'=32,'mp'=8] {'mp'}, use_global_device_ids=true, to_apply=%region_0.0 | all-reduce | flops 196608 | bytes 1179648 | tf_op jit(solution)/shard_map/psum | solution.py:24
  49.2 0.2 fusion.6
  49.4 0.1 convert_element_type.12
  49.5 2.0 %stack.2 = bf16[32,2,2,4096]{3,1,2,0:T(2,128)(2,1)} broadcast(bf16[2,2,4096]{2,0,1:T(2,128)(2,1)S(1)} %copy.16), dimensions={1,2,3} | broadcast | bytes 1081344 | tf_op jit(solution)/shard_map/stack | solution.py:11
  51.5 15.8 %all-to-all-start = ((bf16[32,2,2,4096]{3,1,2,0:T(2,128)(2,1)}), bf16[32,2,2,4096]{3,1,2,0:T(2,128)(2,1)S(1)}, u32[]{:S(2)}, u32[]{:S(2)}) async-start(bf16[32,2,2,4096]{3,1,2,0:T(2,128)(2,1)} %stack.2), calls=%async_computation | async-start | bytes 2097152 | tf_op jit(solution)/shard_map/all_to_all | solution.py:11
  67.3 0.0 copy-done.3
  67.3 0.6 fusion.25
  67.9 28.0 %all-to-all-done = bf16[32,2,2,4096]{3,1,2,0:T(2,128)(2,1)S(1)} async-done(((bf16[32,2,2,4096]{3,1,2,0:T(2,128)(2,1)}), bf16[32,2,2,4096]{3,1,2,0:T(2,128)(2,1)S(1)}, u32[]{:S(2)}, u32[]{:S(2)}) %all-to-all-start) | async-done | bytes 1048608 | tf_op jit(solution)/shard_map/all_to_all | solution.py:11
  95.9 1.9 %copy.17 = bf16[32,2,2,4096]{3,1,0,2:T(2,128)(2,1)} copy(bf16[32,2,2,4096]{3,1,2,0:T(2,128)(2,1)S(1)} %all-to-all-done) | data formatting | bytes 2097152 | tf_op jit(solution)/shard_map/all_to_all | solution.py:11
  97.8 1.5 reshape.15
  99.3 3.0 %fusion.13 = f32[64,256]{1,0:T(8,128)S(1)} fusion(bf16[2,256,4096]{2,1,0:T(8,128)(2,1)} %param.11, bf16[64,2,4096]{2,0,1:T(8,128)(2,1)S(1)} %reshape.15, f32[]{:T(128)} %bitcast.7), kind=kOutput, calls=%fused_computation.10 | convolution fusion | flops 134234112 | bytes 2687488 | tf_op jit(solution)/shard_map/qk,rk->qr/dot_general | solution.py:31
  102.3 3.0 %fusion.10 = f32[64,256]{1,0:T(8,128)S(1)} fusion(f32[64,256]{1,0:T(8,128)S(1)} %fusion.13, bf16[2,256,4096]{2,1,0:T(8,128)(2,1)} %param.11, bf16[64,2,4096]{2,0,1:T(8,128)(2,1)S(1)} %reshape.15, f32[]{:T(128)} %bitcast), kind=kOutput, calls=%fused_computation.9 | convolution fusion | flops 134250496 | bytes 2753024 | tf_op jit(solution)/shard_map/qk,rk->qr/dot_general | solution.py:30
  105.3 0.0 copy-start.2
  105.3 0.3 fusion.20
  105.6 73.6 %psum.15 = f32[64,16]{0,1:T(8,128)S(1)} all-reduce(f32[64,16]{0,1:T(8,128)S(1)} %fusion.20), channel_id=1, replica_groups=mesh['dp'=32,'mp'=8] {'dp','mp'}, use_global_device_ids=true, to_apply=%region_1.0 | all-reduce | flops 1024 | bytes 8192 | tf_op jit(solution)/shard_map/psum | solution.py:37
  179.2 0.6 broadcast_multiply_fusion
  (5 shorter events, 0.1 us)
Async XLA Ops:
  0.6 4.5 %copy-start = (bf16[2,2,384,512]{3,2,1,0:T(8,128)(2,1)S(1)}, bf16[2,2,384,512]{3,2,1,0:T(8,128)(2,1)}, u32[]{:S(2)}) copy-start(bf16[2,2,384,512]{3,2,1,0:T(8,128)(2,1)} %param.8) | copy-start | bytes 4718596
  0.6 4.5 %copy-start.1 = (bf16[512,64]{0,1:T(8,128)(2,1)S(1)}, bf16[512,64]{0,1:T(8,128)(2,1)}, u32[]{:S(2)}) copy-start(bf16[512,64]{0,1:T(8,128)(2,1)} %param.10) | copy-start | bytes 196612
  5.7 61.6 %copy-start.3 = (f32[2]{0:T(128)S(1)}, f32[2]{0:T(128)}, u32[]{:S(2)}) copy-start(f32[2]{0:T(128)} %param.12) | copy-start | bytes 28
  51.5 44.4 %all-to-all-start = ((bf16[32,2,2,4096]{3,1,2,0:T(2,128)(2,1)}), bf16[32,2,2,4096]{3,1,2,0:T(2,128)(2,1)S(1)}, u32[]{:S(2)}, u32[]{:S(2)}) async-start(bf16[32,2,2,4096]{3,1,2,0:T(2,128)(2,1)} %stack.2), calls=%async_computation | async-start | bytes 2097152 | tf_op jit(solution)/shard_map/all_to_all | solution.py:11
  97.8 7.5 %copy-start.4 = (s32[256]{0:T(256)S(1)}, s32[256]{0:T(256)}, u32[]{:S(2)}) copy-start(s32[256]{0:T(256)} %param.13) | copy-start | bytes 3076
  105.3 74.5 %copy-start.2 = (f32[64,256]{1,0:T(8,128)}, f32[64,256]{1,0:T(8,128)S(1)}, u32[]{:S(2)}) copy-start(f32[64,256]{1,0:T(8,128)S(1)} %fusion.10) | copy-start | bytes 196612
